TPU v7x, 512 devices: a whole 4x8x8 slice. The times are simulated.
512 devices in a mesh: seq: 128 (over z, y, core), head: 4 (over x).
Axes of the slice: x: 4, y: 8, z: 8, core: 2. Of those that a mesh axis runs over, the one named last changes fastest.
Arguments:
- hidden: bfloat16 [16384, 1024], P('seq', 'head'), may hold values from -6 to 6
- queries: bfloat16 [16384, 1024], P('seq', 'head'), may hold values from -40 to 40
- suffix_keys: bfloat16 [16384, 1024], P('seq', 'head'), may hold values from -4 to 4
- suffix_values: bfloat16 [16384, 1024], P('seq', 'head'), may hold values from -6 to 6
- lengths: int32 [128], P('seq'), may hold values from 1 to 128, 10240 in all
- key_cache: bfloat16 [128, 32, 1024], P('seq', None, 'head'), may hold values from -6 to 6
- value_cache: bfloat16 [128, 32, 1024], P('seq', None, 'head'), may hold values from -6 to 6
- page_group: int32 [128], replicated, may hold values from 0 to 3, as said below
- out_weight: bfloat16 [1024, 1024], P('head'), may hold values from -0.1875 to 0.1875
- norm_gain: float32 [1024], replicated, may hold values from 0.1 to 1.9
- router_weight: bfloat16 [1024, 16], P('head'), may hold values from -0.1875 to 0.1875
- routes: int32 [16384, 2], P('seq'), may hold values from 0 to 15, all different within a row; in each aligned block of 16 rows (0 to 15, 16 to 31, ...) at most 2 rows name the same one
- gate_weight: bfloat16 [128, 1024, 2816], P('seq', None, 'head'), as said below
- up_weight: bfloat16 [128, 1024, 2816], P('seq', None, 'head'), as said below
- down_weight: bfloat16 [128, 1024, 2816], P('seq', None, 'head'), as said below
- destinations: int32 [128], replicated, may hold values from 0 to 127, as said below
Outputs:
- layer_output: bfloat16 [16384, 1024], P('seq', 'head')
Inputs may be any that keep to these rules, and one draw needn't show every extreme that they name: `lengths`: the largest length is 128. `page_group`: each of the 4 groups is named by exactly 32 entries. `routes`: each row names 2 different experts; in each aligned block of 16 rows no expert is named by more than 2 rows. `gate_weight`: copies h and h2 with h // 8 == h2 // 8 are equal. `up_weight`: copies h and h2 with h // 8 == h2 // 8 are equal. `down_weight`: copies h and h2 with h // 8 == h2 // 8 are equal. `destinations`: A permutation of the requests in which exactly 32 requests change place.
All inputs are finite; a program needn't handle non-finite values. No bound on the sum of `lengths` on one device may be relied on, other than what follows from the above.
Results may differ from a plain program's by a relative error of at most 0.0065.
Values may be sent and summed in bfloat16 or wider, within the bound.
No kernel may reach another device: no remote copies, remote signals or barrier semaphores. Data moves between devices by JAX's collectives and lax.ppermute only.
A program may use at most 64 MiB of HBM per device.

v0:
```python
import jax
import jax.numpy as jnp
from jax import lax
from jax.sharding import PartitionSpec as P

DH = 64
EXPERTS = 16
TOPK = 2
GROUPS = 4
norm_eps = 1e-06


def page_inverse(page_group, group_pages, groups):
    page_total = page_group.shape[0]
    onehot = (page_group[:, None] == jnp.arange(groups, dtype=jnp.int32)[None, :]).astype(jnp.int32)
    page_rank = jnp.sum((jnp.cumsum(onehot, axis=0) - 1) * onehot, axis=1)
    target = page_group * group_pages + page_rank
    return (
        jnp.zeros((page_total,), jnp.int32).at[target].set(jnp.arange(page_total, dtype=jnp.int32))
    )


def attend_rows(query_rows, key_rows, value_rows, prefix_keys, prefix_values, length, head_total):
    row_count = query_rows.shape[0]
    head_size = query_rows.shape[1] // head_total
    scale = head_size ** (-0.5)

    def heads_of(array):
        return array.reshape(array.shape[0], head_total, head_size)

    prefix_scores = (
        jnp.einsum(
            "qhd,khd->hqk",
            heads_of(query_rows),
            heads_of(prefix_keys),
            preferred_element_type=jnp.float32,
        )
        * scale
    )
    suffix_scores = (
        jnp.einsum(
            "qhd,khd->hqk",
            heads_of(query_rows),
            heads_of(key_rows),
            preferred_element_type=jnp.float32,
        )
        * scale
    )
    query_pos = jnp.arange(row_count, dtype=jnp.int32)[:, None]
    key_pos = jnp.arange(row_count, dtype=jnp.int32)[None, :]
    allowed = (key_pos <= query_pos) & (key_pos < length)
    suffix_scores = jnp.where(allowed[None], suffix_scores, -jnp.inf)
    row_max = jnp.maximum(jnp.max(prefix_scores, axis=2), jnp.max(suffix_scores, axis=2))[..., None]
    prefix_exp = jnp.exp(prefix_scores - row_max)
    suffix_exp = jnp.exp(suffix_scores - row_max)
    denominators = jnp.sum(prefix_exp, axis=2, keepdims=True) + jnp.sum(
        suffix_exp, axis=2, keepdims=True
    )
    prefix_probs = (prefix_exp / denominators).astype(jnp.bfloat16)
    suffix_probs = (suffix_exp / denominators).astype(jnp.bfloat16)
    mixed_heads = jnp.einsum(
        "hqk,khd->qhd", prefix_probs, heads_of(prefix_values), preferred_element_type=jnp.float32
    )
    mixed_heads = mixed_heads + jnp.einsum(
        "hqk,khd->qhd", suffix_probs, heads_of(value_rows), preferred_element_type=jnp.float32
    )
    return mixed_heads.reshape(row_count, head_total * head_size).astype(jnp.bfloat16)


def slot_table(route_rows, replicas, per_device, experts):
    row_count, topk_count = route_rows.shape
    sub_rows = row_count // replicas
    flat_routes = route_rows.reshape(replicas, sub_rows * topk_count)
    onehot = (flat_routes[..., None] == jnp.arange(experts, dtype=jnp.int32)).astype(jnp.int32)
    slot_rank = jnp.sum((jnp.cumsum(onehot, axis=1) - 1) * onehot, axis=2).reshape(-1)
    expert_flat = route_rows.reshape(-1)
    block_of = jnp.arange(row_count * topk_count, dtype=jnp.int32) // (sub_rows * topk_count)
    target_device = expert_flat // per_device * replicas + block_of
    local_slot = expert_flat % per_device
    return (target_device, local_slot, slot_rank)


def on_device(
    hidden,
    queries,
    suffix_keys,
    suffix_values,
    lengths,
    key_cache,
    value_cache,
    page_group,
    out_weight,
    norm_gain,
    router_weight,
    routes,
    gate_weight,
    up_weight,
    down_weight,
    destinations,
):
    seq_count = lax.axis_size("seq")
    head_count = lax.axis_size("head")
    seq_index = lax.axis_index("seq")
    head_index = lax.axis_index("head")
    row_count = hidden.shape[0]
    column_width = hidden.shape[1]
    features = queries.shape[1]
    local_heads = features // DH
    block_devices = seq_count // GROUPS
    page_local = key_cache.shape[0]
    page_rows = key_cache.shape[1]
    group_pages = page_local * block_devices
    replicas = max(1, seq_count // EXPERTS)
    per_device = max(1, EXPERTS // seq_count)
    capacity = 5 * row_count * TOPK // (4 * EXPERTS * replicas)
    inverse = page_inverse(page_group, group_pages, GROUPS)
    group_index = seq_index // block_devices
    half_width = page_rows * features
    local_pages = jnp.concatenate(
        [key_cache.reshape(page_local, half_width), value_cache.reshape(page_local, half_width)],
        axis=1,
    )
    all_pages = lax.all_gather(local_pages, "seq", axis=0, tiled=True)
    chosen = lax.dynamic_slice_in_dim(inverse, group_index * group_pages, group_pages, 0)
    held_pages = jnp.take(all_pages, chosen, axis=0)
    prefix_keys = held_pages[:, :half_width].reshape(group_pages * page_rows, features)
    prefix_values = held_pages[:, half_width:].reshape(group_pages * page_rows, features)
    length = lengths[0]
    attended = attend_rows(
        queries, suffix_keys, suffix_values, prefix_keys, prefix_values, length, local_heads
    )
    partial_proj = jnp.dot(attended, out_weight, preferred_element_type=jnp.float32)
    own_columns = lax.dynamic_slice_in_dim(
        partial_proj, head_index * column_width, column_width, 1
    ) + hidden.astype(jnp.float32)
    partial_proj = lax.dynamic_update_slice_in_dim(
        partial_proj, own_columns, head_index * column_width, 1
    )
    resid = lax.psum(partial_proj, "head")
    normed = (
        resid * lax.rsqrt(jnp.mean(resid * resid, axis=1, keepdims=True) + norm_eps) * norm_gain
    ).astype(jnp.bfloat16)
    normed_columns = lax.dynamic_slice_in_dim(normed, head_index * column_width, column_width, 1)
    logits = lax.psum(
        jnp.dot(normed_columns, router_weight, preferred_element_type=jnp.float32), "head"
    )
    chosen_logits = jnp.take_along_axis(logits, routes, axis=1)
    gate_first = jax.nn.sigmoid(chosen_logits[:, 0] - chosen_logits[:, 1])
    gate_second = jax.nn.sigmoid(chosen_logits[:, 1] - chosen_logits[:, 0])
    target_device, local_slot, slot_rank = slot_table(routes, replicas, per_device, EXPERTS)
    token_index = jnp.arange(row_count * TOPK, dtype=jnp.int32) // TOPK
    send_rows = jnp.zeros((seq_count, per_device, capacity, normed.shape[1]), jnp.bfloat16)
    send_rows = send_rows.at[target_device, local_slot, slot_rank].set(
        jnp.take(normed, token_index, axis=0)
    )
    slots = lax.all_to_all(send_rows, "seq", split_axis=0, concat_axis=0, tiled=True)
    gate_act = jnp.einsum("spnd,pdf->spnf", slots, gate_weight, preferred_element_type=jnp.float32)
    up_act = jnp.einsum("spnd,pdf->spnf", slots, up_weight, preferred_element_type=jnp.float32)
    expert_hidden = (jax.nn.gelu(gate_act, approximate=True) * up_act).astype(jnp.bfloat16)
    partial_out = jnp.einsum(
        "spnf,pdf->spnd", expert_hidden, down_weight, preferred_element_type=jnp.float32
    )
    part_dims = partial_out.shape
    split_part = partial_out.reshape(
        part_dims[0], part_dims[1], part_dims[2], head_count, part_dims[3] // head_count
    )
    arrived = lax.all_to_all(
        lax.all_to_all(
            split_part.astype(jnp.bfloat16), "seq", split_axis=0, concat_axis=0, tiled=True
        ),
        "head",
        split_axis=3,
        concat_axis=3,
        tiled=True,
    ).astype(split_part.dtype)
    returned = jnp.sum(arrived, axis=3).astype(jnp.bfloat16)
    picked = (
        returned[target_device, local_slot, slot_rank]
        .astype(jnp.float32)
        .reshape(row_count, TOPK, column_width)
    )
    resid_columns = lax.dynamic_slice_in_dim(resid, head_index * column_width, column_width, 1)
    layer = resid_columns + gate_first[:, None] * picked[:, 0] + gate_second[:, None] * picked[:, 1]
    layer = layer.astype(jnp.bfloat16)
    live_rows = jnp.arange(row_count, dtype=jnp.int32) < length
    layer = jnp.where(live_rows[:, None], layer, jnp.zeros_like(layer))
    out_pieces = layer.reshape(seq_count, row_count // seq_count, column_width)
    scattered = lax.all_to_all(out_pieces, "seq", split_axis=0, concat_axis=0, tiled=True)
    inverse_destination = (
        jnp.zeros((seq_count,), jnp.int32)
        .at[destinations]
        .set(jnp.arange(seq_count, dtype=jnp.int32))
    )
    reordered = jnp.take(scattered, inverse_destination, axis=0)
    settled = lax.all_to_all(reordered, "seq", split_axis=0, concat_axis=0, tiled=True)
    return settled.reshape(row_count, column_width)


def solution(mesh):
    return jax.shard_map(
        on_device,
        mesh=mesh,
        in_specs=(
            P("seq", "head"),
            P("seq", "head"),
            P("seq", "head"),
            P("seq", "head"),
            P("seq"),
            P("seq", None, "head"),
            P("seq", None, "head"),
            P(),
            P("head", None),
            P(),
            P("head", None),
            P("seq", None),
            P("seq", None, "head"),
            P("seq", None, "head"),
            P("seq", None, "head"),
            P(),
        ),
        out_specs=P("seq", "head"),
        check_vma=False,
    )
```

profile of v0, /device:TPU:1, one launch (start us, length us, event | category | flops | bytes accessed | tf_op | source)
XLA Modules:
  0.0 332.7 jit_solution(16132102906732446111)
XLA Ops:
  12.4 1.6 copy.116
  15.8 1.2 compare_select_fusion.6
  17.0 1.0 scatter_custom_fusion.1
  18.9 1.5 fusion.81
  20.4 83.8 %all-gather.3.cloned.1.call-done = bf16[128,1,16384]{2,1,0:T(2,128)(2,1)} async-done(((bf16[1,1,16384]{2,1,0:T(2,128)(2,1)}), bf16[128,1,16384]{2,1,0:T(2,128)(2,1)}) %all-gather.3.cloned.1.call-update) | async-done | bytes 4194320 | tf_op jit(solution)/shard_map/all_gather | solution.py:123
  104.2 9.9 %copy.185 = bf16[128,1,16384]{2,0,1:T(8,128)(2,1)} copy(bf16[128,1,16384]{2,1,0:T(2,128)(2,1)} %all-gather.3.cloned.1.call-done) | data formatting | bytes 8388608
  114.1 4.8 %gather_fusion = bf16[32,16384]{1,0:T(8,128)(2,1)S(1)} fusion(bf16[128,16384]{1,0:T(8,128)(2,1)} %bitcast.164, s32[1024]{0:T(1024)S(1)} %pad_clamp_fusion.2), kind=kCustom, calls=%fused_computation | custom fusion | bytes 2097280 | tf_op jit(solution)/shard_map/jit(_take)/gather | solution.py:125
  120.0 2.1 reshape_reshape.7
  122.1 1.7 bitcast_reduce_fusion
  125.4 3.3 reshape_reshape.6
  129.4 2.0 convolution_bitcast_fusion.1
  133.6 47.2 %all-reduce.2.cloned.1.call-done = f32[128,1024]{1,0:T(8,128)} async-done(((f32[128,1024]{1,0:T(8,128)}), f32[128,1024]{1,0:T(8,128)}) %all-reduce.2.cloned.1.call-update) | async-done | bytes 524304 | tf_op jit(solution)/shard_map/psum | solution.py:139
  180.8 1.2 multiply_reduce_fusion
  182.0 1.2 multiply_convert_fusion
  183.1 1.2 gather_fusion.1
  184.7 15.9 %scatter_fusion = bf16[128,2,1024]{2,1,0:T(2,128)(2,1)S(1)} fusion(bf16[128,2,1024]{2,1,0:T(2,128)(2,1)S(1)} %broadcast.370, s32[256]{0:T(256)S(1)} %bitcast.165, bf16[256,1024]{1,0:T(8,128)(2,1)S(1)} %broadcast_select_fusion.1), kind=kCustom, calls=%fused_computation.7 | custom fusion | bytes 1574912 | tf_op jit(solution)/shard_map/scatter | solution.py:153
  200.6 36.9 %all_to_all.25 = bf16[128,1,2,1024]{3,2,1,0:T(2,128)(2,1)S(1)} all-to-all(bf16[128,1,2,1024]{3,2,1,0:T(2,128)(2,1)S(1)} %bitcast.163), channel_id=1, replica_groups=mesh['seq'=128,'head'=4] {'seq'}, dimensions={0} | all-to-all | bytes 1048576 | tf_op jit(solution)/shard_map/all_to_all | solution.py:156
  237.5 2.0 fusion.42
  239.5 3.2 fusion.23
  243.1 1.0 copy.126
  244.0 5.4 %all-to-all-start.1 = ((bf16[128,1,2,4,256]{4,3,2,1,0:T(4,128)(2,1)}), bf16[128,1,2,4,256]{4,3,2,1,0:T(4,128)(2,1)S(1)}, u32[]{:S(2)}, u32[]{:S(2)}) async-start(bf16[128,1,2,4,256]{4,3,2,1,0:T(4,128)(2,1)} %copy.126), calls=%async_computation.1 | async-start | bytes 1048576 | tf_op jit(solution)/shard_map/all_to_all | solution.py:168
  249.7 1.1 scatter_custom_fusion
  251.0 8.1 %psum.15 = f32[128,16]{0,1:T(8,128)S(1)} all-reduce(f32[128,16]{0,1:T(8,128)S(1)} %fusion.65), channel_id=1, replica_groups=mesh['seq'=128,'head'=4] {'head'}, use_global_device_ids=true, to_apply=%region_10.11 | all-reduce | flops 2048 | bytes 16384 | tf_op jit(solution)/shard_map/psum | solution.py:144
  259.1 2.2 gather_fusion.4
  261.5 8.5 %all-to-all-done.1 = bf16[128,1,2,4,256]{4,3,2,1,0:T(4,128)(2,1)S(1)} async-done(((bf16[128,1,2,4,256]{4,3,2,1,0:T(4,128)(2,1)}), bf16[128,1,2,4,256]{4,3,2,1,0:T(4,128)(2,1)S(1)}, u32[]{:S(2)}, u32[]{:S(2)}) %all-to-all-start.1) | async-done | bytes 524320 | tf_op jit(solution)/shard_map/all_to_all | solution.py:168
  270.9 3.6 %all-to-all-start.2 = ((bf16[128,1,2,4,256]{4,0,2,1,3:T(8,128)(2,1)}), bf16[128,1,2,4,256]{4,0,2,1,3:T(8,128)(2,1)S(1)}, u32[]{:S(2)}, u32[]{:S(2)}) async-start(bf16[128,1,2,4,256]{4,0,2,1,3:T(8,128)(2,1)} %copy.127), calls=%async_computation.2 | async-start | bytes 1048576 | tf_op jit(solution)/shard_map/all_to_all | solution.py:167
  274.6 9.7 %all-to-all-done.2 = bf16[128,1,2,4,256]{4,0,2,1,3:T(8,128)(2,1)S(1)} async-done(((bf16[128,1,2,4,256]{4,0,2,1,3:T(8,128)(2,1)}), bf16[128,1,2,4,256]{4,0,2,1,3:T(8,128)(2,1)S(1)}, u32[]{:S(2)}, u32[]{:S(2)}) %all-to-all-start.2) | async-done | bytes 524320 | tf_op jit(solution)/shard_map/all_to_all | solution.py:167
  284.5 1.6 gather_fusion.2
  286.5 1.0 fusion.63
  289.5 5.8 %all-to-all-start.3 = ((bf16[128,2,128]{2,1,0:T(2,128)(2,1)}), bf16[128,2,128]{2,1,0:T(2,128)(2,1)S(1)}, u32[]{:S(2)}, u32[]{:S(2)}) async-start(bf16[128,2,128]{2,1,0:T(2,128)(2,1)} %reshape.393), calls=%async_computation.3 | async-start | bytes 131072 | tf_op jit(solution)/shard_map/all_to_all | solution.py:188
  295.3 11.5 %all-to-all-done.3 = bf16[128,2,128]{2,1,0:T(2,128)(2,1)S(1)} async-done(((bf16[128,2,128]{2,1,0:T(2,128)(2,1)}), bf16[128,2,128]{2,1,0:T(2,128)(2,1)S(1)}, u32[]{:S(2)}, u32[]{:S(2)}) %all-to-all-start.3) | async-done | bytes 65568 | tf_op jit(solution)/shard_map/all_to_all | solution.py:188
  308.5 16.7 %all_to_all.26 = bf16[128,2,128]{2,1,0:T(2,128)(2,1)S(1)} all-to-all(bf16[128,2,128]{2,1,0:T(2,128)(2,1)S(1)} %reshape.395), channel_id=1, replica_groups=mesh['seq'=128,'head'=4] {'seq'}, dimensions={0} | all-to-all | bytes 131072 | tf_op jit(solution)/shard_map/all_to_all | solution.py:195
  (102 shorter events, 20.4 us)
Async XLA Ops:
  6.5 233.0 %copy-start = (bf16[1,1024,704]{1,2,0:T(8,128)(2,1)S(1)}, bf16[1,1024,704]{1,2,0:T(8,128)(2,1)}, u32[]{:S(2)}) copy-start(bf16[1,1024,704]{1,2,0:T(8,128)(2,1)} %param.30) | copy-start | bytes 4325380
  6.5 97.7 %all-gather.3.cloned.1.call-start = ((), (), s32[]{:S(2)}) async-start(), calls=%async_computation.6 | async-start | bytes 8454144 | tf_op jit(solution)/shard_map/all_gather | solution.py:123
  8.9 171.9 %all-reduce.2.cloned.1.call-start = ((), (), s32[]{:S(2)}) async-start(), calls=%async_computation.5 | async-start | bytes 1048576 | tf_op jit(solution)/shard_map/psum | solution.py:139
  10.8 103.3 %copy-start.4 = (bf16[128,256]{0,1:T(8,128)(2,1)}, bf16[128,256]{0,1:T(8,128)(2,1)S(1)}, u32[]{:S(2)}) copy-start(bf16[128,256]{0,1:T(8,128)(2,1)S(1)} %copy.111) | copy-start | bytes 196612
  18.0 96.1 %copy-start.14 = (pred[128]{0:T(512)(128)(4,1)}, pred[128]{0:T(512)(128)(4,1)S(1)}, u32[]{:S(2)}) copy-start(pred[128]{0:T(512)(128)(4,1)S(1)} %iota_compare_fusion.4) | copy-start | bytes 388
  122.1 1.7 copy-start.11
  122.1 2.7 copy-start.2
  123.8 1.6 copy-start.8
  129.4 2.0 copy-start.3
  129.4 2.0 copy-start.7
  129.4 2.1 copy-start.9
  129.4 2.3 copy-start.5
  131.4 0.8 copy-start.6
  131.4 1.7 copy-start.10
  131.4 50.6 %copy-start.13 = (f32[1024]{0:T(1024)S(1)}, f32[1024]{0:T(1024)}, u32[]{:S(2)}) copy-start(f32[1024]{0:T(1024)} %param.25) | copy-start | bytes 12292
  132.3 0.8 copy-start.1
  242.7 8.2 %copy-start.12 = (bf16[256,16]{0,1:T(8,128)(2,1)S(1)}, bf16[256,16]{0,1:T(8,128)(2,1)}, u32[]{:S(2)}) copy-start(bf16[256,16]{0,1:T(8,128)(2,1)} %param.26) | copy-start | bytes 24580
  244.0 26.0 %all-to-all-start.1 = ((bf16[128,1,2,4,256]{4,3,2,1,0:T(4,128)(2,1)}), bf16[128,1,2,4,256]{4,3,2,1,0:T(4,128)(2,1)S(1)}, u32[]{:S(2)}, u32[]{:S(2)}) async-start(bf16[128,1,2,4,256]{4,3,2,1,0:T(4,128)(2,1)} %copy.126), calls=%async_computation.1 | async-start | bytes 1048576 | tf_op jit(solution)/shard_map/all_to_all | solution.py:168
  270.9 15.5 %copy-start.15 = (pred[128]{0:T(512)(128)(4,1)S(1)}, pred[128]{0:T(512)(128)(4,1)}, u32[]{:S(2)}) copy-start(pred[128]{0:T(512)(128)(4,1)} %copy-done.14) | copy-start | bytes 388
  270.9 13.3 %all-to-all-start.2 = ((bf16[128,1,2,4,256]{4,0,2,1,3:T(8,128)(2,1)}), bf16[128,1,2,4,256]{4,0,2,1,3:T(8,128)(2,1)S(1)}, u32[]{:S(2)}, u32[]{:S(2)}) async-start(bf16[128,1,2,4,256]{4,0,2,1,3:T(8,128)(2,1)} %copy.127), calls=%async_computation.2 | async-start | bytes 1048576 | tf_op jit(solution)/shard_map/all_to_all | solution.py:167
  289.5 17.3 %all-to-all-start.3 = ((bf16[128,2,128]{2,1,0:T(2,128)(2,1)}), bf16[128,2,128]{2,1,0:T(2,128)(2,1)S(1)}, u32[]{:S(2)}, u32[]{:S(2)}) async-start(bf16[128,2,128]{2,1,0:T(2,128)(2,1)} %reshape.393), calls=%async_computation.3 | async-start | bytes 131072 | tf_op jit(solution)/shard_map/all_to_all | solution.py:188
Sparse Core Ops, SparseCore 0:
  10.5 93.6 all-gather.2
  133.2 47.5 all-reduce.1
where the time goes:
time: 334 us; the launch traced here: 333 us
  waiting for transfers between devices  161 us (48%)
  blocking collectives  61.7 us (18%)
  local copies, waits for them, and re-layouts  57.8 us (17%)
  starting transfers between devices  14.9 us (4%)
  between operations  14.6 us (4%)
  other arithmetic  12.1 us (4%)
  matrix products  10.9 us (3%)
    all_gather x1, waiting for transfers between devices, on_device(): all_pages = lax.all_gather(local_pages, 'seq', axis=0, tiled=True)  83.8 us
    psum x1, waiting for transfers between devices, on_device(): resid = lax.psum(partial_proj, 'head')  47.2 us
    all_to_all x1, blocking collectives, on_device(): lax.all_to_all(send_rows, 'seq', split_axis=0, concat_axis=0, tiled=True)  36.9 us
    unnamed x45, local copies, waits for them, and re-layouts  18.3 us
    all_to_all x1, blocking collectives, on_device(): lax.all_to_all(reordered, 'seq', split_axis=0, concat_axis=0, tiled=True)  16.7 us
    scatter x1, local copies, waits for them, and re-layouts, on_device(): send_rows.at[target_device, local_slot, slot_rank]  15.9 us
    all_to_all x1, waiting for transfers between devices, on_device(): lax.all_to_all(out_pieces, 'seq', split_axis=0, concat_axis=0, tiled=True)  11.5 us
    all_to_all x1, waiting for transfers between devices, on_device(): lax.all_to_all(lax.all_to_all(split_part.astype(jnp.bfloat16), 'seq', spl...  9.7 us
  transfers between devices with their start and end apart: 5, of which 5 were waited for; matrix products, arithmetic and copies ran while one was open for 5% of the time, Pallas kernels for 0%

commit v1 on v0

--- a/solution.py
+++ b/solution.py
@@ -8,6 +8,14 @@
 TOPK = 2
 GROUPS = 4
 norm_eps = 1e-06
+
+
+def doubling_sum(x, name):
+    count, total = (lax.axis_size(name), x)
+    for far in [1 << k for k in range(count.bit_length() - 1)]:
+        swap = [(i, i ^ far) for i in range(count)]
+        total = total + lax.ppermute(total, name, swap)
+    return total
 
 
 def page_inverse(page_group, group_pages, groups):
@@ -136,7 +144,7 @@
     partial_proj = lax.dynamic_update_slice_in_dim(
         partial_proj, own_columns, head_index * column_width, 1
     )
-    resid = lax.psum(partial_proj, "head")
+    resid = doubling_sum(partial_proj, "head")
     normed = (
         resid * lax.rsqrt(jnp.mean(resid * resid, axis=1, keepdims=True) + norm_eps) * norm_gain
     ).astype(jnp.bfloat16)

time: 334 us -> 307 us (0.919)
  waiting for transfers between devices: 161 us -> 136 us
  starting transfers between devices: 14.9 us -> 23.3 us
  blocking collectives: 61.7 us -> 56.9 us
  other arithmetic: 12.1 us -> 7.4 us
    psum x1 -> x0, waiting for transfers between devices: 47.2 us -> none  [on_device(): resid = lax.psum(partial_proj, 'head')]
    ppermute x0 -> x2, waiting for transfers between devices: none -> 21.5 us  [doubling_sum(): total = total + lax.ppermute(total, name, swap)]
    ppermute x0 -> x2, starting transfers between devices: none -> 7.89 us  [doubling_sum(): total = total + lax.ppermute(total, name, swap)]
    all_to_all x1, blocking collectives: 36.9 us -> 31.1 us  [on_device(): lax.all_to_all(send_rows, 'seq', split_axis=0, concat_axis=0, tiled=True)]
    unnamed x45 -> x33, local copies, waits for them, and re-layouts: 18.3 us -> 16.8 us
  transfers between devices with their start and end apart: 5 -> 6, of which waited for: 5 -> 6; matrix products, arithmetic and copies ran while one was open for 5% -> 4% of each run, Pallas kernels for 0% -> 0%
where the time goes in v1:
time: 307 us; the launch traced here: 306 us
  waiting for transfers between devices  136 us (44%)
  blocking collectives  56.9 us (19%)
  local copies, waits for them, and re-layouts  56.1 us (18%)
  starting transfers between devices  23.3 us (8%)
  between operations  14.5 us (5%)
  matrix products  11.4 us (4%)
  other arithmetic  7.4 us (2%)
    all_gather x1, waiting for transfers between devices, on_device(): all_pages = lax.all_gather(local_pages, 'seq', axis=0, tiled=True)  86 us
    all_to_all x1, blocking collectives, on_device(): lax.all_to_all(send_rows, 'seq', split_axis=0, concat_axis=0, tiled=True)  31.1 us
    ppermute x2, waiting for transfers between devices, doubling_sum(): total = total + lax.ppermute(total, name, swap)  21.5 us
    unnamed x33, local copies, waits for them, and re-layouts  16.8 us
    all_to_all x1, blocking collectives, on_device(): lax.all_to_all(reordered, 'seq', split_axis=0, concat_axis=0, tiled=True)  16.7 us
    scatter x1, local copies, waits for them, and re-layouts, on_device(): send_rows.at[target_device, local_slot, slot_rank]  15.9 us
    all_to_all x1, waiting for transfers between devices, on_device(): lax.all_to_all(out_pieces, 'seq', split_axis=0, concat_axis=0, tiled=True)  11.5 us
    all_to_all x1, waiting for transfers between devices, on_device(): lax.all_to_all(lax.all_to_all(split_part.astype(jnp.bfloat16), 'seq', spl...  9.52 us
  transfers between devices with their start and end apart: 6, of which 6 were waited for; matrix products, arithmetic and copies ran while one was open for 4% of the time, Pallas kernels for 0%

profile of v1, /device:TPU:1, one launch (start us, length us, event | category | flops | bytes accessed | tf_op | source)
XLA Modules:
  0.0 305.9 jit_solution(3304283626580576685)
XLA Ops:
  11.4 1.0 copy.113
  12.4 1.6 copy.116
  14.8 1.3 compare_select_fusion.6
  16.0 1.0 scatter_custom_fusion.1
  18.2 86.0 %all-gather.3.cloned.1.call-done = bf16[128,1,16384]{2,1,0:T(2,128)(2,1)} async-done(((bf16[1,1,16384]{2,1,0:T(2,128)(2,1)}), bf16[128,1,16384]{2,1,0:T(2,128)(2,1)}) %all-gather.3.cloned.1.call-update) | async-done | bytes 4194320 | tf_op jit(solution)/shard_map/all_gather | solution.py:131
  104.2 9.9 %copy.185 = bf16[128,1,16384]{2,0,1:T(8,128)(2,1)} copy(bf16[128,1,16384]{2,1,0:T(2,128)(2,1)} %all-gather.3.cloned.1.call-done) | data formatting | bytes 8388608
  114.1 4.8 %gather_fusion = bf16[32,16384]{1,0:T(8,128)(2,1)S(1)} fusion(bf16[128,16384]{1,0:T(8,128)(2,1)} %bitcast.164, s32[1024]{0:T(1024)S(1)} %pad_clamp_fusion.2), kind=kCustom, calls=%fused_computation | custom fusion | bytes 2097280 | tf_op jit(solution)/shard_map/jit(_take)/gather | solution.py:133
  120.0 2.1 reshape_reshape.7
  122.1 1.7 bitcast_reduce_fusion
  124.3 3.3 %reshape_reshape.6 = bf16[1024,4,64]{2,1,0:T(4,128)(2,1)} reshape(bf16[32,8192]{1,0:T(8,128)(2,1)} %get-tuple-element.12) | data formatting | bytes 1048576 | tf_op jit(solution)/shard_map/reshape;reshape | solution.py:37
  127.5 2.0 convolution_bitcast_fusion.1
  130.4 3.3 %collective-permute-start = (f32[128,1024]{1,0:T(8,128)S(1)}, f32[128,1024]{1,0:T(8,128)S(1)}, u32[]{:S(2)}, u32[]{:S(2)}) collective-permute-start(f32[128,1024]{1,0:T(8,128)S(1)} %add_dynamic-update-slice_fusion), channel_id=1, source_target_pairs={{0,1},{1,0},{2,3},{3,2},{4,5},{5,4},{6,7},{7,6},{8,9},{9,8},{10,11... | collective-permute-start | bytes 1572872 | tf_op jit(solution)/shard_map/ppermute | solution.py:17
  134.7 10.8 %collective-permute-done = f32[128,1024]{1,0:T(8,128)S(1)} collective-permute-done((f32[128,1024]{1,0:T(8,128)S(1)}, f32[128,1024]{1,0:T(8,128)S(1)}, u32[]{:S(2)}, u32[]{:S(2)}) %collective-permute-start) | collective-permute-done | bytes 524320 | tf_op jit(solution)/shard_map/ppermute | solution.py:17
  145.6 4.6 %collective-permute-start.1 = (f32[128,1024]{1,0:T(8,128)S(1)}, f32[128,1024]{1,0:T(8,128)S(1)}, u32[]{:S(2)}, u32[]{:S(2)}) collective-permute-start(f32[128,1024]{1,0:T(8,128)S(1)} %add.187), channel_id=1, source_target_pairs={{0,2},{1,3},{2,0},{3,1},{4,6},{5,7},{6,4},{7,5},{8,10},{9,11},{10,... | collective-permute-start | bytes 1572872 | tf_op jit(solution)/shard_map/ppermute | solution.py:17
  150.7 10.7 %collective-permute-done.1 = f32[128,1024]{1,0:T(8,128)S(1)} collective-permute-done((f32[128,1024]{1,0:T(8,128)S(1)}, f32[128,1024]{1,0:T(8,128)S(1)}, u32[]{:S(2)}, u32[]{:S(2)}) %collective-permute-start.1) | collective-permute-done | bytes 524320 | tf_op jit(solution)/shard_map/ppermute | solution.py:17
  161.6 1.2 gather_fusion.1
  163.2 15.9 %scatter_fusion = bf16[128,2,1024]{2,1,0:T(2,128)(2,1)S(1)} fusion(bf16[128,2,1024]{2,1,0:T(2,128)(2,1)S(1)} %broadcast.370, s32[256]{0:T(256)S(1)} %bitcast.165, bf16[256,1024]{1,0:T(8,128)(2,1)S(1)} %broadcast_select_fusion.1), kind=kCustom, calls=%fused_computation.7 | custom fusion | bytes 1574912 | tf_op jit(solution)/shard_map/scatter | solution.py:161
  179.1 31.1 %all_to_all.25 = bf16[128,1,2,1024]{3,2,1,0:T(2,128)(2,1)S(1)} all-to-all(bf16[128,1,2,1024]{3,2,1,0:T(2,128)(2,1)S(1)} %bitcast.163), channel_id=1, replica_groups=mesh['seq'=128,'head'=4] {'seq'}, dimensions={0} | all-to-all | bytes 1048576 | tf_op jit(solution)/shard_map/all_to_all | solution.py:164
  210.2 2.9 fusion.42
  213.0 3.3 %fusion.23 = bf16[128,1,2,1024]{3,0,2,1:T(8,128)(2,1)S(1)} fusion(bf16[1,1024,704]{1,2,0:T(8,128)(2,1)S(1)} %copy-done, f32[128,1,2,704]{0,3,2,1:T(8,128)} %fusion.42, bf16[1,1024,704]{1,2,0:T(8,128)(2,1)} %param.29, bf16[128,1,2,1024]{3,2,1,0:T(2,128)(2,1)S(1)} %all_to_all.25), kind=kOutput, calls=%fused_computation.25 | convolution fusion | flops 738820096 | bytes 4653056 | tf_op jit(solution)/shard_map/spnf,pdf->spnd/dot_general | solution.py:168
  216.8 1.0 copy.126
  217.7 5.4 %all-to-all-start.1 = ((bf16[128,1,2,4,256]{4,3,2,1,0:T(4,128)(2,1)}), bf16[128,1,2,4,256]{4,3,2,1,0:T(4,128)(2,1)S(1)}, u32[]{:S(2)}, u32[]{:S(2)}) async-start(bf16[128,1,2,4,256]{4,3,2,1,0:T(4,128)(2,1)} %copy.126), calls=%async_computation.1 | async-start | bytes 1048576 | tf_op jit(solution)/shard_map/all_to_all | solution.py:176
  223.4 1.1 scatter_custom_fusion
  224.7 9.1 %psum.7 = f32[128,16]{0,1:T(8,128)S(1)} all-reduce(f32[128,16]{0,1:T(8,128)S(1)} %fusion.65), channel_id=1, replica_groups=mesh['seq'=128,'head'=4] {'head'}, use_global_device_ids=true, to_apply=%region_9.10 | all-reduce | flops 2048 | bytes 16384 | tf_op jit(solution)/shard_map/psum | solution.py:152
  233.8 2.0 gather_fusion.4
  236.0 7.7 %all-to-all-done.1 = bf16[128,1,2,4,256]{4,3,2,1,0:T(4,128)(2,1)S(1)} async-done(((bf16[128,1,2,4,256]{4,3,2,1,0:T(4,128)(2,1)}), bf16[128,1,2,4,256]{4,3,2,1,0:T(4,128)(2,1)S(1)}, u32[]{:S(2)}, u32[]{:S(2)}) %all-to-all-start.1) | async-done | bytes 524320 | tf_op jit(solution)/shard_map/all_to_all | solution.py:176
  244.6 4.0 %all-to-all-start.2 = ((bf16[128,1,2,4,256]{4,0,2,1,3:T(8,128)(2,1)}), bf16[128,1,2,4,256]{4,0,2,1,3:T(8,128)(2,1)S(1)}, u32[]{:S(2)}, u32[]{:S(2)}) async-start(bf16[128,1,2,4,256]{4,0,2,1,3:T(8,128)(2,1)} %copy.127), calls=%async_computation.2 | async-start | bytes 1048576 | tf_op jit(solution)/shard_map/all_to_all | solution.py:175
  248.6 9.5 %all-to-all-done.2 = bf16[128,1,2,4,256]{4,0,2,1,3:T(8,128)(2,1)S(1)} async-done(((bf16[128,1,2,4,256]{4,0,2,1,3:T(8,128)(2,1)}), bf16[128,1,2,4,256]{4,0,2,1,3:T(8,128)(2,1)S(1)}, u32[]{:S(2)}, u32[]{:S(2)}) %all-to-all-start.2) | async-done | bytes 524320 | tf_op jit(solution)/shard_map/all_to_all | solution.py:175
  258.3 1.6 gather_fusion.2
  262.4 6.0 %all-to-all-start.3 = ((bf16[128,2,128]{2,1,0:T(2,128)(2,1)}), bf16[128,2,128]{2,1,0:T(2,128)(2,1)S(1)}, u32[]{:S(2)}, u32[]{:S(2)}) async-start(bf16[128,2,128]{2,1,0:T(2,128)(2,1)} %reshape.393), calls=%async_computation.3 | async-start | bytes 131072 | tf_op jit(solution)/shard_map/all_to_all | solution.py:196
  268.4 11.5 %all-to-all-done.3 = bf16[128,2,128]{2,1,0:T(2,128)(2,1)S(1)} async-done(((bf16[128,2,128]{2,1,0:T(2,128)(2,1)}), bf16[128,2,128]{2,1,0:T(2,128)(2,1)S(1)}, u32[]{:S(2)}, u32[]{:S(2)}) %all-to-all-start.3) | async-done | bytes 65568 | tf_op jit(solution)/shard_map/all_to_all | solution.py:196
  281.7 16.7 %all_to_all.26 = bf16[128,2,128]{2,1,0:T(2,128)(2,1)S(1)} all-to-all(bf16[128,2,128]{2,1,0:T(2,128)(2,1)S(1)} %reshape.395), channel_id=1, replica_groups=mesh['seq'=128,'head'=4] {'seq'}, dimensions={0} | all-to-all | bytes 131072 | tf_op jit(solution)/shard_map/all_to_all | solution.py:203
  (92 shorter events, 17.5 us)
Async XLA Ops:
  6.5 206.5 %copy-start = (bf16[1,1024,704]{1,2,0:T(8,128)(2,1)S(1)}, bf16[1,1024,704]{1,2,0:T(8,128)(2,1)}, u32[]{:S(2)}) copy-start(bf16[1,1024,704]{1,2,0:T(8,128)(2,1)} %param.30) | copy-start | bytes 4325380
  6.5 97.7 %all-gather.3.cloned.1.call-start = ((), (), s32[]{:S(2)}) async-start(), calls=%async_computation.5 | async-start | bytes 8454144 | tf_op jit(solution)/shard_map/all_gather | solution.py:131
  10.8 103.3 %copy-start.3 = (bf16[128,256]{0,1:T(8,128)(2,1)}, bf16[128,256]{0,1:T(8,128)(2,1)S(1)}, u32[]{:S(2)}) copy-start(bf16[128,256]{0,1:T(8,128)(2,1)S(1)} %copy.111) | copy-start | bytes 196612
  122.1 2.1 copy-start.1
  127.5 2.0 copy-start.2
  127.5 2.0 copy-start.6
  127.5 2.2 copy-start.4
  129.5 0.8 copy-start.5
  129.5 4.1 %copy-start.7 = (s32[128,2]{0,1:T(2,128)S(1)}, s32[128,2]{0,1:T(2,128)}, u32[]{:S(2)}) copy-start(s32[128,2]{0,1:T(2,128)} %param.27) | copy-start | bytes 3076
  130.4 31.1 %copy-start.9 = (f32[1024]{0:T(1024)S(1)}, f32[1024]{0:T(1024)}, u32[]{:S(2)}) copy-start(f32[1024]{0:T(1024)} %param.25) | copy-start | bytes 12292
  130.4 15.1 %collective-permute-start = (f32[128,1024]{1,0:T(8,128)S(1)}, f32[128,1024]{1,0:T(8,128)S(1)}, u32[]{:S(2)}, u32[]{:S(2)}) collective-permute-start(f32[128,1024]{1,0:T(8,128)S(1)} %add_dynamic-update-slice_fusion), channel_id=1, source_target_pairs={{0,1},{1,0},{2,3},{3,2},{4,5},{5,4},{6,7},{7,6},{8,9},{9,8},{10,11... | collective-permute-start | bytes 1572872 | tf_op jit(solution)/shard_map/ppermute | solution.py:17
  145.6 15.7 %collective-permute-start.1 = (f32[128,1024]{1,0:T(8,128)S(1)}, f32[128,1024]{1,0:T(8,128)S(1)}, u32[]{:S(2)}, u32[]{:S(2)}) collective-permute-start(f32[128,1024]{1,0:T(8,128)S(1)} %add.187), channel_id=1, source_target_pairs={{0,2},{1,3},{2,0},{3,1},{4,6},{5,7},{6,4},{7,5},{8,10},{9,11},{10,... | collective-permute-start | bytes 1572872 | tf_op jit(solution)/shard_map/ppermute | solution.py:17
  216.4 8.2 %copy-start.8 = (bf16[256,16]{0,1:T(8,128)(2,1)S(1)}, bf16[256,16]{0,1:T(8,128)(2,1)}, u32[]{:S(2)}) copy-start(bf16[256,16]{0,1:T(8,128)(2,1)} %param.26) | copy-start | bytes 24580
  217.7 26.0 %all-to-all-start.1 = ((bf16[128,1,2,4,256]{4,3,2,1,0:T(4,128)(2,1)}), bf16[128,1,2,4,256]{4,3,2,1,0:T(4,128)(2,1)S(1)}, u32[]{:S(2)}, u32[]{:S(2)}) async-start(bf16[128,1,2,4,256]{4,3,2,1,0:T(4,128)(2,1)} %copy.126), calls=%async_computation.1 | async-start | bytes 1048576 | tf_op jit(solution)/shard_map/all_to_all | solution.py:176
  244.6 13.5 %all-to-all-start.2 = ((bf16[128,1,2,4,256]{4,0,2,1,3:T(8,128)(2,1)}), bf16[128,1,2,4,256]{4,0,2,1,3:T(8,128)(2,1)S(1)}, u32[]{:S(2)}, u32[]{:S(2)}) async-start(bf16[128,1,2,4,256]{4,0,2,1,3:T(8,128)(2,1)} %copy.127), calls=%async_computation.2 | async-start | bytes 1048576 | tf_op jit(solution)/shard_map/all_to_all | solution.py:175
  262.4 17.6 %all-to-all-start.3 = ((bf16[128,2,128]{2,1,0:T(2,128)(2,1)}), bf16[128,2,128]{2,1,0:T(2,128)(2,1)S(1)}, u32[]{:S(2)}, u32[]{:S(2)}) async-start(bf16[128,2,128]{2,1,0:T(2,128)(2,1)} %reshape.393), calls=%async_computation.3 | async-start | bytes 131072 | tf_op jit(solution)/shard_map/all_to_all | solution.py:196
Sparse Core Ops, SparseCore 0:
  10.5 93.6 all-gather.2
